TPU v7x, 512 devices: a whole 4x4x16 slice. The times are simulated.
512 devices in a mesh: dp: 32 (over z, core), expert: 16 (over x, y).
Axes of the slice: x: 4, y: 4, z: 16, core: 2. Of those that a mesh axis runs over, the one named last changes fastest.
Arguments:
- grad_out: bfloat16 [65536, 2048], P(('dp', 'expert')), may hold values from -6 to 6
- gate: float32 [65536, 1], P(('dp', 'expert')), may hold values from 0.25 to 1
- expert_ids: int32 [65536, 1], P(('dp', 'expert')), may hold values from 0 to 15; in each aligned block of 128 rows (0 to 127, 128 to 255, ...) at most 10 rows name the same one
- w_in: bfloat16 [16, 5120, 2048], P('expert', 'dp'), may hold values from -0.125 to 0.125
- w_out: bfloat16 [16, 5120, 2048], P('expert', 'dp'), may hold values from -0.078125 to 0.078125
- pre_act: bfloat16 [32, 16, 160, 5120], P('dp', 'expert'), may hold values from -6 to 6
Outputs:
- grad_in: bfloat16 [65536, 2048], P(('dp', 'expert'))
Inputs may be any that keep to these rules, and one draw needn't show every extreme that they name: `expert_ids`: among the 128 tokens of one device no expert is named more than 10 times, and in every draw some device names some expert exactly 10 times.
All inputs are finite; a program needn't handle non-finite values.
Results may differ from a plain program's by a relative error of at most 0.0057.
Values may be sent and summed in bfloat16 or wider, within the bound.
No kernel may reach another device: no remote copies, remote signals or barrier semaphores. Data moves between devices by JAX's collectives and lax.ppermute only.
A program may use at most 192 MiB of HBM per device.

v0:
```python
import jax
import jax.numpy as jnp
from jax import lax
from jax.sharding import PartitionSpec as P


def gelu_slope(values):
    inside = 0.7978845608028654 * (values + 0.044715 * values * values * values)
    curved = jnp.tanh(inside)
    return 0.5 * (1.0 + curved) + 0.5 * values * (1.0 - curved * curved) * 0.7978845608028654 * (
        1.0 + 3.0 * 0.044715 * values * values
    )


def body(grad_out, gate, expert_ids, w_in, w_out, pre_act):
    groups = lax.axis_size("expert")
    slots = pre_act.shape[2]
    capacity = slots // groups
    width = grad_out.shape[1]
    chosen = expert_ids[:, 0]
    hit_table = (chosen[:, None] == jnp.arange(groups, dtype=jnp.int32)[None, :]).astype(jnp.int32)
    position = jnp.sum(jnp.cumsum(hit_table, axis=0) * hit_table, axis=1) - 1
    target = chosen * capacity + position
    scaled = (grad_out.astype(jnp.float32) * gate).astype(jnp.bfloat16)
    outgoing = (
        jnp.zeros((slots, width), jnp.bfloat16)
        .at[target]
        .set(scaled)
        .reshape(groups, capacity, width)
    )
    arrived = lax.all_to_all(outgoing, "expert", split_axis=0, concat_axis=0, tiled=True)
    rows_in = arrived.reshape(slots, width)
    stashed = pre_act[0, 0]
    hidden_grad = jnp.einsum(
        "sd,fd->sf",
        rows_in,
        lax.all_gather(w_out, "dp", axis=1, tiled=True)[0],
        preferred_element_type=jnp.float32,
    )
    act_grad = (hidden_grad * gelu_slope(stashed.astype(jnp.float32))).astype(jnp.bfloat16)
    slot_sum = jnp.einsum(
        "sf,fd->sd",
        act_grad,
        lax.all_gather(w_in, "dp", axis=1, tiled=True)[0],
        preferred_element_type=jnp.float32,
    )
    slot_grad = slot_sum.astype(jnp.bfloat16).reshape(groups, capacity, width)
    returned = lax.all_to_all(slot_grad, "expert", split_axis=0, concat_axis=0, tiled=True)
    return returned.reshape(slots, width)[target]


def solution(mesh):
    return jax.shard_map(
        body,
        mesh=mesh,
        in_specs=(
            P(("dp", "expert"), None),
            P(("dp", "expert"), None),
            P(("dp", "expert"), None),
            P("expert", "dp", None),
            P("expert", "dp", None),
            P("dp", "expert", None, None),
        ),
        out_specs=P(("dp", "expert"), None),
        check_vma=False,
    )
```

profile of v0, /device:TPU:8, one launch (start us, length us, event | category | flops | bytes accessed | tf_op | source)
XLA Modules:
  0.0 312.6 jit_solution(17426288469553297094)
XLA Ops:
  6.5 0.0 all-gather.3.cloned.1.call-start
  6.5 0.7 all-gather.3.cloned.1.call-update
  7.3 0.0 all-gather.5.cloned.1.call-start
  7.3 0.7 all-gather.5.cloned.1.call-update
  8.0 0.7 fusion.23
  8.8 0.2 reduce_window_sum.11
  8.9 0.8 select_reduce_fusion
  9.8 0.7 fusion.24
  10.4 2.1 scatter_custom_fusion
  12.5 0.2 reshape.23
  12.8 22.9 %all_to_all.10 = bf16[16,10,2048]{2,1,0:T(8,128)(2,1)S(1)} all-to-all(bf16[16,10,2048]{2,1,0:T(8,128)(2,1)S(1)} %reshape.23), channel_id=1, replica_groups=mesh['dp'=32,'expert'=16] {'expert'}, dimensions={0} | all-to-all | bytes 1310720 | tf_op jit(solution)/shard_map/all_to_all | solution.py:31
  35.7 0.2 reshape.24
  35.9 105.8 %all-gather.3.cloned.1.call-done = bf16[1,5120,2048]{2,1,0:T(8,128)(2,1)} async-done(((bf16[1,160,2048]{2,1,0:T(8,128)(2,1)}), bf16[1,5120,2048]{2,1,0:T(8,128)(2,1)}) %all-gather.3.cloned.1.call-update) | async-done | bytes 20971536 | tf_op jit(solution)/shard_map/all_gather | solution.py:37
  141.7 12.6 %fusion.7 = bf16[160,5120]{1,0:T(8,128)(2,1)S(1)} fusion(bf16[160,2048]{1,0:T(8,128)(2,1)S(1)} %reshape.24, bf16[1,5120,2048]{2,1,0:T(8,128)(2,1)} %all-gather.3.cloned.1.call-done, bf16[1,1,160,5120]{3,2,1,0:T(8,128)(2,1)} %param.11), kind=kOutput, calls=%fused_computation.14 | convolution fusion | flops 3371827200 | bytes 24903680 | tf_op jit(solution)/shard_map/sd,fd->sf/dot_general | solution.py:34
  154.3 115.2 %all-gather.5.cloned.1.call-done = bf16[1,5120,2048]{2,1,0:T(8,128)(2,1)} async-done(((bf16[1,160,2048]{2,1,0:T(8,128)(2,1)}), bf16[1,5120,2048]{2,1,0:T(8,128)(2,1)}) %all-gather.5.cloned.1.call-update) | async-done | bytes 20971536 | tf_op jit(solution)/shard_map/all_gather | solution.py:44
  269.5 9.0 %fusion.17 = bf16[160,2048]{1,0:T(8,128)(2,1)S(1)} fusion(bf16[160,5120]{1,0:T(8,128)(2,1)S(1)} %fusion.7, bf16[1,5120,2048]{2,1,0:T(8,128)(2,1)} %all-gather.5.cloned.1.call-done), kind=kOutput, calls=%fused_computation.22 | convolution fusion | flops 3355770880 | bytes 23265280 | tf_op jit(solution)/shard_map/sf,fd->sd/dot_general | solution.py:41
  278.5 1.2 reshape.25
  279.7 7.3 %all-to-all-start.1 = ((bf16[16,10,2048]{2,1,0:T(8,128)(2,1)}), bf16[16,10,2048]{2,1,0:T(8,128)(2,1)S(1)}, u32[]{:S(2)}, u32[]{:S(2)}) async-start(bf16[16,10,2048]{2,1,0:T(8,128)(2,1)} %reshape.25), calls=%async_computation.1 | async-start | bytes 2097152 | tf_op jit(solution)/shard_map/all_to_all | solution.py:48
  287.0 16.8 %all-to-all-done.1 = bf16[16,10,2048]{2,1,0:T(8,128)(2,1)S(1)} async-done(((bf16[16,10,2048]{2,1,0:T(8,128)(2,1)}), bf16[16,10,2048]{2,1,0:T(8,128)(2,1)S(1)}, u32[]{:S(2)}, u32[]{:S(2)}) %all-to-all-start.1) | async-done | bytes 655392 | tf_op jit(solution)/shard_map/all_to_all | solution.py:48
  303.8 0.2 reshape.26
  304.0 1.7 gather_fusion
  (1 shorter events, 0.0 us)
Async XLA Ops:
  6.5 135.2 %all-gather.3.cloned.1.call-start = ((), (), s32[]{:S(2)}) async-start(), calls=%async_computation.2 | async-start | bytes 21626880 | tf_op jit(solution)/shard_map/all_gather | solution.py:37
  7.3 262.3 %all-gather.5.cloned.1.call-start = ((), (), s32[]{:S(2)}) async-start(), calls=%async_computation.3 | async-start | bytes 21626880 | tf_op jit(solution)/shard_map/all_gather | solution.py:44
  279.7 24.1 %all-to-all-start.1 = ((bf16[16,10,2048]{2,1,0:T(8,128)(2,1)}), bf16[16,10,2048]{2,1,0:T(8,128)(2,1)S(1)}, u32[]{:S(2)}, u32[]{:S(2)}) async-start(bf16[16,10,2048]{2,1,0:T(8,128)(2,1)} %reshape.25), calls=%async_computation.1 | async-start | bytes 2097152 | tf_op jit(solution)/shard_map/all_to_all | solution.py:48
Sparse Core Ops, SparseCore 0:
  9.5 132.2 all-gather.2
  143.8 125.6 all-gather.4
where the time goes:
time: 313 us
  waiting for transfers between devices  239 us (76%)
  blocking collectives  22.9 us (7%)
  matrix products  21.6 us (7%)
  between operations  13.5 us (4%)
  starting transfers between devices  7.29 us (2%)
  other arithmetic  4.53 us (1%)
  local copies, waits for them, and re-layouts  3.59 us (1%)
    all_gather x1, waiting for transfers between devices, body(): lax.all_gather(w_in, 'dp', axis=1, tiled=True)[0]  115 us
    all_gather x1, waiting for transfers between devices, body(): lax.all_gather(w_out, 'dp', axis=1, tiled=True)[0]  106 us
    all_to_all x1, blocking collectives, body(): lax.all_to_all(outgoing, 'expert', split_axis=0, concat_axis=0, tiled=True)  22.9 us
    all_to_all x1, waiting for transfers between devices, body(): lax.all_to_all(slot_grad, 'expert', split_axis=0, concat_axis=0, tiled=True)  16.8 us
    dot_general x1, matrix products, body(): jnp.einsum('sd,fd->sf', rows_in, lax.all_gather(w_out, 'dp', axis=1, tile...  12.6 us
    dot_general x1, matrix products, body(): jnp.einsum('sf,fd->sd', act_grad, lax.all_gather(w_in, 'dp', axis=1, tile...  8.95 us
    all_to_all x1, starting transfers between devices, body(): lax.all_to_all(slot_grad, 'expert', split_axis=0, concat_axis=0, tiled=True)  7.25 us
  transfers between devices with their start and end apart: 3, of which 3 were waited for; matrix products, arithmetic and copies ran while one was open for 6% of the time, Pallas kernels for 0%

commit v1 on v0

--- a/solution.py
+++ b/solution.py
@@ -31,17 +31,21 @@
     arrived = lax.all_to_all(outgoing, "expert", split_axis=0, concat_axis=0, tiled=True)
     rows_in = arrived.reshape(slots, width)
     stashed = pre_act[0, 0]
+    shards = lax.axis_size("dp")
+    rows = w_out.shape[1]
+    both = jnp.concatenate([w_out, w_in], axis=1)
+    gathered = lax.all_gather(both, "dp", axis=1, tiled=True).reshape(shards, 2, rows, width)
     hidden_grad = jnp.einsum(
-        "sd,fd->sf",
+        "sd,gfd->sgf",
         rows_in,
-        lax.all_gather(w_out, "dp", axis=1, tiled=True)[0],
+        gathered[:, 0],
         preferred_element_type=jnp.float32,
-    )
+    ).reshape(slots, shards * rows)
     act_grad = (hidden_grad * gelu_slope(stashed.astype(jnp.float32))).astype(jnp.bfloat16)
     slot_sum = jnp.einsum(
-        "sf,fd->sd",
-        act_grad,
-        lax.all_gather(w_in, "dp", axis=1, tiled=True)[0],
+        "sgf,gfd->sd",
+        act_grad.reshape(slots, shards, rows),
+        gathered[:, 1],
         preferred_element_type=jnp.float32,
     )
     slot_grad = slot_sum.astype(jnp.bfloat16).reshape(groups, capacity, width)

time: 313 us -> 329 us (1.051)
  local copies, waits for them, and re-layouts: 3.59 us -> 25.8 us
  waiting for transfers between devices: 239 us -> 230 us
    slice x0 -> x1, local copies, waits for them, and re-layouts: none -> 17.8 us  [body(): gathered[:, 0]]
    all_gather x2 -> x1, waiting for transfers between devices: 221 us -> 213 us  [body(): lax.all_gather(both, 'dp', axis=1, tiled=True)]
    reshape x0 -> x1, local copies, waits for them, and re-layouts: none -> 4.44 us  [body(): act_grad.reshape(slots, shards, rows)]
  transfers between devices with their start and end apart: 3 -> 2, of which waited for: 3 -> 2; matrix products, arithmetic and copies ran while one was open for 6% -> 1% of each run, Pallas kernels for 0% -> 0%
where the time goes in v1:
time: 329 us; the launch traced here: 328 us
  waiting for transfers between devices  230 us (70%)
  local copies, waits for them, and re-layouts  25.8 us (8%)
  matrix products  24.7 us (8%)
  blocking collectives  22.9 us (7%)
  between operations  13.5 us (4%)
  starting transfers between devices  7.26 us (2%)
  other arithmetic  4.6 us (1%)
    all_gather x1, waiting for transfers between devices, body(): lax.all_gather(both, 'dp', axis=1, tiled=True)  213 us
    all_to_all x1, blocking collectives, body(): lax.all_to_all(outgoing, 'expert', split_axis=0, concat_axis=0, tiled=True)  22.9 us
    slice x1, local copies, waits for them, and re-layouts, body(): gathered[:, 0]  17.8 us
    all_to_all x1, waiting for transfers between devices, body(): lax.all_to_all(slot_grad, 'expert', split_axis=0, concat_axis=0, tiled=True)  16.8 us
    dot_general x1, matrix products, body(): jnp.einsum('sd,gfd->sgf', rows_in, gathered[:, 0], preferred_element_type...  13.3 us
    dot_general x1, matrix products, body(): jnp.einsum('sgf,gfd->sd', act_grad.reshape(slots, shards, rows), gathered...  11.4 us
    all_to_all x1, starting transfers between devices, body(): lax.all_to_all(slot_grad, 'expert', split_axis=0, concat_axis=0, tiled=True)  7.26 us
  transfers between devices with their start and end apart: 2, of which 2 were waited for; matrix products, arithmetic and copies ran while one was open for 1% of the time, Pallas kernels for 0%

profile of v1, /device:TPU:8, one launch (start us, length us, event | category | flops | bytes accessed | tf_op | source)
XLA Modules:
  0.0 328.3 jit_solution(9330431443200145467)
XLA Ops:
  6.5 0.0 copy-start.1
  6.5 0.0 copy-start.2
  6.5 0.0 copy-start
  6.5 0.0 all-gather.2.cloned.1.call-start
  6.5 2.5 pad_maximum_fusion
  9.1 0.0 all-gather.2.cloned.1.call-update
  9.1 0.0 copy-done.1
  9.1 0.1 fusion.19
  9.2 0.2 reduce_window_sum.11
  9.4 0.2 select_reduce_fusion
  9.6 0.0 copy-done.2
  9.6 0.0 copy-done
  9.6 1.6 scatter_custom_fusion
  11.2 0.2 reshape.32
  11.4 22.9 %all_to_all.10 = bf16[16,10,2048]{2,1,0:T(8,128)(2,1)S(1)} all-to-all(bf16[16,10,2048]{2,1,0:T(8,128)(2,1)S(1)} %reshape.32), channel_id=1, replica_groups=mesh['dp'=32,'expert'=16] {'expert'}, dimensions={0} | all-to-all | bytes 1310720 | tf_op jit(solution)/shard_map/all_to_all | solution.py:31
  34.4 0.2 reshape.33
  34.6 212.7 %all-gather.2.cloned.1.call-done = bf16[1,10240,2048]{2,1,0:T(8,128)(2,1)} async-done(((bf16[1,320,2048]{2,1,0:T(8,128)(2,1)}), bf16[1,10240,2048]{2,1,0:T(8,128)(2,1)}) %all-gather.2.cloned.1.call-update) | async-done | bytes 41943056 | tf_op jit(solution)/shard_map/all_gather | solution.py:37
  247.3 0.0 copy-start.3
  247.3 17.8 %slice.10 = bf16[32,1,160,2048]{3,2,1,0:T(8,128)(2,1)} slice(bf16[32,2,160,2048]{3,2,1,0:T(8,128)(2,1)} %bitcast.29), slice={[0:32], [0:1], [0:160], [0:2048]} | slice | bytes 41943040 | tf_op jit(solution)/shard_map/slice | solution.py:41
  265.0 0.0 copy-done.3
  265.0 13.3 %fusion.1 = bf16[160,5120]{1,0:T(8,128)(2,1)} fusion(bf16[160,2048]{1,0:T(8,128)(2,1)S(1)} %reshape.33, bf16[5120,2048]{1,0:T(8,128)(2,1)} %bitcast.28, bf16[1,1,160,5120]{3,2,1,0:T(8,128)(2,1)S(1)} %copy-done.3), kind=kOutput, calls=%fused_computation.12 | convolution fusion | flops 3371827200 | bytes 24903680 | tf_op jit(solution)/shard_map/sd,gfd->sgf/dot_general | solution.py:38
  278.3 4.4 %reshape.35 = bf16[160,32,160]{2,1,0:T(8,128)(2,1)S(1)} reshape(bf16[160,5120]{1,0:T(8,128)(2,1)} %fusion.1) | data formatting | bytes 3276800 | tf_op jit(solution)/shard_map/reshape | solution.py:47
  282.8 11.4 %fusion.13 = bf16[160,2048]{1,0:T(8,128)(2,1)S(1)} fusion(bf16[32,2,160,2048]{3,2,1,0:T(8,128)(2,1)} %bitcast.30, bf16[160,32,160]{2,1,0:T(8,128)(2,1)S(1)} %reshape.35), kind=kOutput, calls=%fused_computation.22 | convolution fusion | flops 3355770880 | bytes 23265280 | tf_op jit(solution)/shard_map/sgf,gfd->sd/dot_general | solution.py:45
  294.2 1.2 reshape.36
  295.4 7.3 %all-to-all-start.1 = ((bf16[16,10,2048]{2,1,0:T(8,128)(2,1)}), bf16[16,10,2048]{2,1,0:T(8,128)(2,1)S(1)}, u32[]{:S(2)}, u32[]{:S(2)}) async-start(bf16[16,10,2048]{2,1,0:T(8,128)(2,1)} %reshape.36), calls=%async_computation.1 | async-start | bytes 2097152 | tf_op jit(solution)/shard_map/all_to_all | solution.py:52
  302.7 16.8 %all-to-all-done.1 = bf16[16,10,2048]{2,1,0:T(8,128)(2,1)S(1)} async-done(((bf16[16,10,2048]{2,1,0:T(8,128)(2,1)}), bf16[16,10,2048]{2,1,0:T(8,128)(2,1)S(1)}, u32[]{:S(2)}, u32[]{:S(2)}) %all-to-all-start.1) | async-done | bytes 655392 | tf_op jit(solution)/shard_map/all_to_all | solution.py:52
  319.5 0.2 reshape.37
  319.8 1.7 gather_fusion
  (2 shorter events, 0.0 us)
Async XLA Ops:
  6.5 2.6 copy-start.1
  6.5 3.0 copy-start.2
  6.5 3.1 copy-start
  6.5 240.7 %all-gather.2.cloned.1.call-start = ((), (), s32[]{:S(2)}) async-start(), calls=%async_computation.2 | async-start | bytes 43253760 | tf_op jit(solution)/shard_map/all_gather | solution.py:37
  247.3 17.8 %copy-start.3 = (bf16[1,1,160,5120]{3,2,1,0:T(8,128)(2,1)S(1)}, bf16[1,1,160,5120]{3,2,1,0:T(8,128)(2,1)}, u32[]{:S(2)}) copy-start(bf16[1,1,160,5120]{3,2,1,0:T(8,128)(2,1)} %param.11) | copy-start | bytes 4915204
  295.4 24.1 %all-to-all-start.1 = ((bf16[16,10,2048]{2,1,0:T(8,128)(2,1)}), bf16[16,10,2048]{2,1,0:T(8,128)(2,1)S(1)}, u32[]{:S(2)}, u32[]{:S(2)}) async-start(bf16[16,10,2048]{2,1,0:T(8,128)(2,1)} %reshape.36), calls=%async_computation.1 | async-start | bytes 2097152 | tf_op jit(solution)/shard_map/all_to_all | solution.py:52
Sparse Core Ops, SparseCore 0:
  9.5 237.7 all-gather.1

commit v2 on v1

--- a/solution.py
+++ b/solution.py
@@ -1,6 +1,8 @@
 import jax
 import jax.numpy as jnp
 from jax import lax
+from jax.experimental import pallas as pl
+from jax.experimental.pallas import tpu as pltpu
 from jax.sharding import PartitionSpec as P
 
 
@@ -10,6 +12,53 @@
     return 0.5 * (1.0 + curved) + 0.5 * values * (1.0 - curved * curved) * 0.7978845608028654 * (
         1.0 + 3.0 * 0.044715 * values * values
     )
+
+
+def expert_kernel(rows_ref, pre_ref, w_ref, out_ref, acc_ref):
+    step = pl.program_id(0)
+    group, _, rows, width = w_ref.shape
+
+    @pl.when(step == 0)
+    def _():
+        acc_ref[...] = jnp.zeros_like(acc_ref)
+
+    w_out = w_ref[:, 0].reshape(group * rows, width)
+    w_in = w_ref[:, 1].reshape(group * rows, width)
+    hidden = lax.dot_general(
+        rows_ref[...], w_out, (((1,), (1,)), ((), ())), preferred_element_type=jnp.float32
+    )
+    act = (hidden * gelu_slope(pre_ref[...].astype(jnp.float32))).astype(jnp.bfloat16)
+    acc_ref[...] += jnp.dot(act, w_in, preferred_element_type=jnp.float32)
+
+    @pl.when(step == pl.num_programs(0) - 1)
+    def _():
+        out_ref[...] = acc_ref[...].astype(out_ref.dtype)
+
+
+def expert_pass(rows_in, stashed, gathered, group=4):
+    shards, _, rows, width = gathered.shape
+    slots = rows_in.shape[0]
+    steps = shards // group
+    return pl.pallas_call(
+        expert_kernel,
+        grid=(steps,),
+        in_specs=[
+            pl.BlockSpec((slots, width), lambda g: (0, 0)),
+            pl.BlockSpec((slots, group * rows), lambda g: (0, g)),
+            pl.BlockSpec((group, 2, rows, width), lambda g: (g, 0, 0, 0)),
+        ],
+        out_specs=pl.BlockSpec((slots, width), lambda g: (0, 0)),
+        out_shape=jax.ShapeDtypeStruct((slots, width), jnp.bfloat16),
+        scratch_shapes=[pltpu.VMEM((slots, width), jnp.float32)],
+        compiler_params=pltpu.CompilerParams(
+            dimension_semantics=("arbitrary",), vmem_limit_bytes=48 * 1024 * 1024
+        ),
+        cost_estimate=pl.CostEstimate(
+            flops=4 * slots * shards * rows * width,
+            transcendentals=slots * shards * rows,
+            bytes_accessed=2 * (gathered.size + stashed.size + 2 * rows_in.size),
+        ),
+    )(rows_in, stashed, gathered)
 
 
 def body(grad_out, gate, expert_ids, w_in, w_out, pre_act):
@@ -35,20 +84,7 @@
     rows = w_out.shape[1]
     both = jnp.concatenate([w_out, w_in], axis=1)
     gathered = lax.all_gather(both, "dp", axis=1, tiled=True).reshape(shards, 2, rows, width)
-    hidden_grad = jnp.einsum(
-        "sd,gfd->sgf",
-        rows_in,
-        gathered[:, 0],
-        preferred_element_type=jnp.float32,
-    ).reshape(slots, shards * rows)
-    act_grad = (hidden_grad * gelu_slope(stashed.astype(jnp.float32))).astype(jnp.bfloat16)
-    slot_sum = jnp.einsum(
-        "sgf,gfd->sd",
-        act_grad.reshape(slots, shards, rows),
-        gathered[:, 1],
-        preferred_element_type=jnp.float32,
-    )
-    slot_grad = slot_sum.astype(jnp.bfloat16).reshape(groups, capacity, width)
+    slot_grad = expert_pass(rows_in, stashed, gathered).reshape(groups, capacity, width)
     returned = lax.all_to_all(slot_grad, "expert", split_axis=0, concat_axis=0, tiled=True)
     return returned.reshape(slots, width)[target]
 

time: 329 us -> 302 us (0.918)
  matrix products: 24.7 us -> 0 us
  local copies, waits for them, and re-layouts: 25.8 us -> 4.78 us
  Pallas kernels: 0 us -> 20 us
    dot_general x2 -> x0, matrix products: 24.7 us -> none  [the longest x1 13.3 us: body(): jnp.einsum('sd,gfd->sgf', rows_in, gathered[:, 0], preferred_element_type...]
    pallas_call x0 -> x1, Pallas kernels: none -> 20 us  [expert_pass(): pl.pallas_call(expert_kernel, grid=(steps,), in_specs=[pl.BlockSpec((slot...]
    slice x1 -> x0, local copies, waits for them, and re-layouts: 17.8 us -> none  [body(): gathered[:, 0]]
    reshape x2 -> x1, local copies, waits for them, and re-layouts: 5.63 us -> 1.19 us  [body(): expert_pass(rows_in, stashed, gathered).reshape(groups, capacity, width)]
where the time goes in v2:
time: 302 us; the launch traced here: 301 us
  waiting for transfers between devices  228 us (75%)
  blocking collectives  23.2 us (8%)
  Pallas kernels  20 us (7%)
  between operations  13.5 us (4%)
  starting transfers between devices  7.26 us (2%)
  local copies, waits for them, and re-layouts  4.78 us (2%)
  other arithmetic  4.6 us (2%)
    all_gather x1, waiting for transfers between devices, body(): lax.all_gather(both, 'dp', axis=1, tiled=True)  211 us
    all_to_all x1, blocking collectives, body(): lax.all_to_all(outgoing, 'expert', split_axis=0, concat_axis=0, tiled=True)  23.2 us
    pallas_call x1, Pallas kernels, expert_pass(): pl.pallas_call(expert_kernel, grid=(steps,), in_specs=[pl.BlockSpec((slot...  20 us
    all_to_all x1, waiting for transfers between devices, body(): lax.all_to_all(slot_grad, 'expert', split_axis=0, concat_axis=0, tiled=True)  16.8 us
    all_to_all x1, starting transfers between devices, body(): lax.all_to_all(slot_grad, 'expert', split_axis=0, concat_axis=0, tiled=True)  7.25 us
  transfers between devices with their start and end apart: 2, of which 2 were waited for; matrix products, arithmetic and copies ran while one was open for 1% of the time, Pallas kernels for 0%

profile of v2, /device:TPU:8, one launch (start us, length us, event | category | flops | bytes accessed | tf_op | source)
XLA Modules:
  0.0 301.4 jit_solution(9188727321780699023)
XLA Ops:
  6.5 0.0 copy-start.2
  6.5 0.0 copy-start.3
  6.5 0.0 copy-start.1
  6.5 0.0 all-gather.2.cloned.1.call-start
  6.5 2.5 pad_maximum_fusion
  9.1 0.0 all-gather.2.cloned.1.call-update
  9.1 0.0 copy-done.2
  9.1 0.1 fusion.3
  9.2 0.2 reduce_window_sum.11
  9.4 0.2 select_reduce_fusion
  9.6 0.0 copy-done.3
  9.6 0.0 copy-done.1
  9.6 1.6 scatter_custom_fusion
  11.2 0.2 reshape.24
  11.4 0.0 copy-start
  11.4 23.2 %all_to_all.10 = bf16[16,10,2048]{2,1,0:T(8,128)(2,1)} all-to-all(bf16[16,10,2048]{2,1,0:T(8,128)(2,1)S(1)} %reshape.24), channel_id=1, replica_groups=mesh['dp'=32,'expert'=16] {'expert'}, dimensions={0} | all-to-all | bytes 1310720 | tf_op jit(solution)/shard_map/all_to_all | solution.py:80
  34.6 1.4 reshape.25.rows_ref
  36.0 211.2 %all-gather.2.cloned.1.call-done = bf16[1,10240,2048]{2,1,0:T(8,128)(2,1)} async-done(((bf16[1,320,2048]{2,1,0:T(8,128)(2,1)}), bf16[1,10240,2048]{2,1,0:T(8,128)(2,1)}) %all-gather.2.cloned.1.call-update) | async-done | bytes 41943056 | tf_op jit(solution)/shard_map/all_gather | solution.py:86
  247.3 0.0 copy-done
  247.3 20.0 %shard_map.64 = bf16[160,2048]{1,0:T(8,128)(2,1)S(1)} custom-call(bf16[160,2048]{1,0:T(8,128)(2,1)S(1)} %reshape.25.rows_ref, bf16[160,5120]{1,0:T(8,128)(2,1)S(1)} %bitcast.10, bf16[32,2,160,2048]{3,2,1,0:T(8,128)(2,1)} %bitcast.11), custom_call_target="tpu_custom_call" | custom-call | flops 6710886400 | bytes 44892160 | tf_op jit(solution)/shard_map/pallas_call | solution.py:42
  267.3 1.2 reshape.27
  268.5 7.3 %all-to-all-start.1 = ((bf16[16,10,2048]{2,1,0:T(8,128)(2,1)}), bf16[16,10,2048]{2,1,0:T(8,128)(2,1)S(1)}, u32[]{:S(2)}, u32[]{:S(2)}) async-start(bf16[16,10,2048]{2,1,0:T(8,128)(2,1)} %reshape.27), calls=%async_computation.1 | async-start | bytes 2097152 | tf_op jit(solution)/shard_map/all_to_all | solution.py:88
  275.8 16.8 %all-to-all-done.1 = bf16[16,10,2048]{2,1,0:T(8,128)(2,1)S(1)} async-done(((bf16[16,10,2048]{2,1,0:T(8,128)(2,1)}), bf16[16,10,2048]{2,1,0:T(8,128)(2,1)S(1)}, u32[]{:S(2)}, u32[]{:S(2)}) %all-to-all-start.1) | async-done | bytes 655392 | tf_op jit(solution)/shard_map/all_to_all | solution.py:88
  292.6 0.2 reshape.28
  292.8 1.7 gather_fusion
  (2 shorter events, 0.0 us)
Async XLA Ops:
  6.5 2.6 copy-start.2
  6.5 3.0 %copy-start.3 = (f32[128,1]{0,1:T(1,128)S(1)}, f32[128,1]{0,1:T(1,128)}, u32[]{:S(2)}) copy-start(f32[128,1]{0,1:T(1,128)} %param.7) | copy-start | bytes 1540
  6.5 3.1 %copy-start.1 = (bf16[128,2048]{1,0:T(8,128)(2,1)S(1)}, bf16[128,2048]{1,0:T(8,128)(2,1)}, u32[]{:S(2)}) copy-start(bf16[128,2048]{1,0:T(8,128)(2,1)} %param.6) | copy-start | bytes 1572868
  6.5 240.7 %all-gather.2.cloned.1.call-start = ((), (), s32[]{:S(2)}) async-start(), calls=%async_computation.2 | async-start | bytes 43253760 | tf_op jit(solution)/shard_map/all_gather | solution.py:86
  11.4 235.8 %copy-start = (bf16[1,1,160,5120]{3,2,1,0:T(8,128)(2,1)S(1)}, bf16[1,1,160,5120]{3,2,1,0:T(8,128)(2,1)}, u32[]{:S(2)}) copy-start(bf16[1,1,160,5120]{3,2,1,0:T(8,128)(2,1)} %param.11) | copy-start | bytes 4915204
  268.5 24.1 %all-to-all-start.1 = ((bf16[16,10,2048]{2,1,0:T(8,128)(2,1)}), bf16[16,10,2048]{2,1,0:T(8,128)(2,1)S(1)}, u32[]{:S(2)}, u32[]{:S(2)}) async-start(bf16[16,10,2048]{2,1,0:T(8,128)(2,1)} %reshape.27), calls=%async_computation.1 | async-start | bytes 2097152 | tf_op jit(solution)/shard_map/all_to_all | solution.py:88
Sparse Core Ops, SparseCore 0:
  9.5 237.7 all-gather.1

commit v3 on v2

--- a/solution.py
+++ b/solution.py
@@ -35,7 +35,7 @@
         out_ref[...] = acc_ref[...].astype(out_ref.dtype)
 
 
-def expert_pass(rows_in, stashed, gathered, group=4):
+def expert_pass(rows_in, stashed, gathered, group=8):
     shards, _, rows, width = gathered.shape
     slots = rows_in.shape[0]
     steps = shards // group
@@ -71,22 +71,17 @@
     position = jnp.sum(jnp.cumsum(hit_table, axis=0) * hit_table, axis=1) - 1
     target = chosen * capacity + position
     scaled = (grad_out.astype(jnp.float32) * gate).astype(jnp.bfloat16)
-    outgoing = (
-        jnp.zeros((slots, width), jnp.bfloat16)
-        .at[target]
-        .set(scaled)
-        .reshape(groups, capacity, width)
-    )
+    outgoing = jnp.zeros((slots, width), jnp.bfloat16).at[target].set(scaled)
     arrived = lax.all_to_all(outgoing, "expert", split_axis=0, concat_axis=0, tiled=True)
-    rows_in = arrived.reshape(slots, width)
+    rows_in = arrived
     stashed = pre_act[0, 0]
     shards = lax.axis_size("dp")
     rows = w_out.shape[1]
     both = jnp.concatenate([w_out, w_in], axis=1)
     gathered = lax.all_gather(both, "dp", axis=1, tiled=True).reshape(shards, 2, rows, width)
-    slot_grad = expert_pass(rows_in, stashed, gathered).reshape(groups, capacity, width)
+    slot_grad = expert_pass(rows_in, stashed, gathered)
     returned = lax.all_to_all(slot_grad, "expert", split_axis=0, concat_axis=0, tiled=True)
-    return returned.reshape(slots, width)[target]
+    return returned[target]
 
 
 def solution(mesh):

time: 302 us -> 299 us (0.990)
    all_to_all x0 -> x4, local copies, waits for them, and re-layouts: none -> 3.04 us  [the longest x2 1.62 us: body(): lax.all_to_all(outgoing, 'expert', split_axis=0, concat_axis=0, tiled=True)]
    reshape x4 -> x0, local copies, waits for them, and re-layouts: 3.04 us -> none  [the longest x1 1.41 us: body(): rows_in = arrived.reshape(slots, width)]
where the time goes in v3:
time: 299 us
  waiting for transfers between devices  228 us (76%)
  blocking collectives  23.2 us (8%)
  Pallas kernels  17.6 us (6%)
  between operations  13.5 us (5%)
  starting transfers between devices  7.25 us (2%)
  local copies, waits for them, and re-layouts  4.78 us (2%)
  other arithmetic  4.6 us (2%)
    all_gather x1, waiting for transfers between devices, body(): lax.all_gather(both, 'dp', axis=1, tiled=True)  211 us
    all_to_all x1, blocking collectives, body(): lax.all_to_all(outgoing, 'expert', split_axis=0, concat_axis=0, tiled=True)  23.2 us
    pallas_call x1, Pallas kernels, expert_pass(): pl.pallas_call(expert_kernel, grid=(steps,), in_specs=[pl.BlockSpec((slot...  17.6 us
    all_to_all x1, waiting for transfers between devices, body(): lax.all_to_all(slot_grad, 'expert', split_axis=0, concat_axis=0, tiled=True)  16.8 us
    all_to_all x1, starting transfers between devices, body(): lax.all_to_all(slot_grad, 'expert', split_axis=0, concat_axis=0, tiled=True)  7.25 us
  transfers between devices with their start and end apart: 2, of which 2 were waited for; matrix products, arithmetic and copies ran while one was open for 1% of the time, Pallas kernels for 0%

profile of v3, /device:TPU:8, one launch (start us, length us, event | category | flops | bytes accessed | tf_op | source)
XLA Modules:
  0.0 299.0 jit_solution(16049993767875067359)
XLA Ops:
  6.5 0.0 copy-start.2
  6.5 0.0 copy-start.3
  6.5 0.0 copy-start.1
  6.5 0.0 all-gather.2.cloned.1.call-start
  6.5 2.5 pad_maximum_fusion
  9.1 0.0 all-gather.2.cloned.1.call-update
  9.1 0.0 copy-done.2
  9.1 0.1 fusion.3
  9.2 0.2 reduce_window_sum.11
  9.4 0.2 select_reduce_fusion
  9.6 0.0 copy-done.3
  9.6 0.0 copy-done.1
  9.6 1.6 scatter_custom_fusion
  11.2 0.2 all_to_all.15
  11.4 0.0 copy-start
  11.4 23.2 %all_to_all.23 = bf16[16,10,2048]{2,1,0:T(8,128)(2,1)} all-to-all(bf16[16,10,2048]{2,1,0:T(8,128)(2,1)S(1)} %all_to_all.15), channel_id=1, replica_groups=mesh['dp'=32,'expert'=16] {'expert'}, dimensions={0} | all-to-all | bytes 1310720 | tf_op jit(solution)/shard_map/all_to_all | solution.py:75
  34.6 1.4 all_to_all.17.rows_ref
  36.0 211.2 %all-gather.2.cloned.1.call-done = bf16[1,10240,2048]{2,1,0:T(8,128)(2,1)} async-done(((bf16[1,320,2048]{2,1,0:T(8,128)(2,1)}), bf16[1,10240,2048]{2,1,0:T(8,128)(2,1)}) %all-gather.2.cloned.1.call-update) | async-done | bytes 41943056 | tf_op jit(solution)/shard_map/all_gather | solution.py:81
  247.3 0.0 copy-done
  247.3 17.6 %shard_map.64 = bf16[160,2048]{1,0:T(8,128)(2,1)S(1)} custom-call(bf16[160,2048]{1,0:T(8,128)(2,1)S(1)} %all_to_all.17.rows_ref, bf16[160,5120]{1,0:T(8,128)(2,1)S(1)} %bitcast.10, bf16[32,2,160,2048]{3,2,1,0:T(8,128)(2,1)} %bitcast.11), custom_call_target="tpu_custom_call" | custom-call | flops 6710886400 | bytes 44892160 | tf_op jit(solution)/shard_map/pallas_call | solution.py:42
  264.9 1.2 all_to_all.18
  266.1 7.2 %all-to-all-start.1 = ((bf16[16,10,2048]{2,1,0:T(8,128)(2,1)}), bf16[16,10,2048]{2,1,0:T(8,128)(2,1)S(1)}, u32[]{:S(2)}, u32[]{:S(2)}) async-start(bf16[16,10,2048]{2,1,0:T(8,128)(2,1)} %all_to_all.18), calls=%async_computation.1 | async-start | bytes 2097152 | tf_op jit(solution)/shard_map/all_to_all | solution.py:83
  273.3 16.8 %all-to-all-done.1 = bf16[16,10,2048]{2,1,0:T(8,128)(2,1)S(1)} async-done(((bf16[16,10,2048]{2,1,0:T(8,128)(2,1)}), bf16[16,10,2048]{2,1,0:T(8,128)(2,1)S(1)}, u32[]{:S(2)}, u32[]{:S(2)}) %all-to-all-start.1) | async-done | bytes 655392 | tf_op jit(solution)/shard_map/all_to_all | solution.py:83
  290.2 0.2 all_to_all.20
  290.4 1.7 gather_fusion
  (2 shorter events, 0.0 us)
Async XLA Ops:
  6.5 2.6 copy-start.2
  6.5 3.0 %copy-start.3 = (f32[128,1]{0,1:T(1,128)S(1)}, f32[128,1]{0,1:T(1,128)}, u32[]{:S(2)}) copy-start(f32[128,1]{0,1:T(1,128)} %param.7) | copy-start | bytes 1540
  6.5 3.1 %copy-start.1 = (bf16[128,2048]{1,0:T(8,128)(2,1)S(1)}, bf16[128,2048]{1,0:T(8,128)(2,1)}, u32[]{:S(2)}) copy-start(bf16[128,2048]{1,0:T(8,128)(2,1)} %param.6) | copy-start | bytes 1572868
  6.5 240.7 %all-gather.2.cloned.1.call-start = ((), (), s32[]{:S(2)}) async-start(), calls=%async_computation.2 | async-start | bytes 43253760 | tf_op jit(solution)/shard_map/all_gather | solution.py:81
  11.4 235.8 %copy-start = (bf16[1,1,160,5120]{3,2,1,0:T(8,128)(2,1)S(1)}, bf16[1,1,160,5120]{3,2,1,0:T(8,128)(2,1)}, u32[]{:S(2)}) copy-start(bf16[1,1,160,5120]{3,2,1,0:T(8,128)(2,1)} %param.11) | copy-start | bytes 4915204
  266.1 24.1 %all-to-all-start.1 = ((bf16[16,10,2048]{2,1,0:T(8,128)(2,1)}), bf16[16,10,2048]{2,1,0:T(8,128)(2,1)S(1)}, u32[]{:S(2)}, u32[]{:S(2)}) async-start(bf16[16,10,2048]{2,1,0:T(8,128)(2,1)} %all_to_all.18), calls=%async_computation.1 | async-start | bytes 2097152 | tf_op jit(solution)/shard_map/all_to_all | solution.py:83
Sparse Core Ops, SparseCore 0:
  9.5 237.7 all-gather.1

commit v4 on v3

--- a/solution.py
+++ b/solution.py
@@ -51,7 +51,7 @@
         out_shape=jax.ShapeDtypeStruct((slots, width), jnp.bfloat16),
         scratch_shapes=[pltpu.VMEM((slots, width), jnp.float32)],
         compiler_params=pltpu.CompilerParams(
-            dimension_semantics=("arbitrary",), vmem_limit_bytes=48 * 1024 * 1024
+            dimension_semantics=("arbitrary",), vmem_limit_bytes=60 * 1024 * 1024
         ),
         cost_estimate=pl.CostEstimate(
             flops=4 * slots * shards * rows * width,

time: 299 us -> 302 us (1.010)
  no operation moved by 1% of the time
where the time goes in v4:
time: 302 us; the launch traced here: 301 us
  waiting for transfers between devices  229 us (76%)
  blocking collectives  22.9 us (8%)
  Pallas kernels  18.9 us (6%)
  between operations  13.5 us (4%)
  starting transfers between devices  7.26 us (2%)
  local copies, waits for them, and re-layouts  5.45 us (2%)
  other arithmetic  4.62 us (2%)
    all_gather x1, waiting for transfers between devices, body(): lax.all_gather(both, 'dp', axis=1, tiled=True)  212 us
    all_to_all x1, blocking collectives, body(): lax.all_to_all(outgoing, 'expert', split_axis=0, concat_axis=0, tiled=True)  22.9 us
    pallas_call x1, Pallas kernels, expert_pass(): pl.pallas_call(expert_kernel, grid=(steps,), in_specs=[pl.BlockSpec((slot...  18.9 us
    all_to_all x1, waiting for transfers between devices, body(): lax.all_to_all(slot_grad, 'expert', split_axis=0, concat_axis=0, tiled=True)  16.8 us
    all_to_all x1, starting transfers between devices, body(): lax.all_to_all(slot_grad, 'expert', split_axis=0, concat_axis=0, tiled=True)  7.25 us
  transfers between devices with their start and end apart: 2, of which 2 were waited for; matrix products, arithmetic and copies ran while one was open for 1% of the time, Pallas kernels for 0%

profile of v4, /device:TPU:8, one launch (start us, length us, event | category | flops | bytes accessed | tf_op | source)
XLA Modules:
  0.0 301.3 jit_solution(15206099378233272137)
XLA Ops:
  6.5 0.0 copy-start.1
  6.5 0.0 copy-start.2
  6.5 0.0 copy-start
  6.5 0.0 all-gather.2.cloned.1.call-start
  6.5 2.6 pad_maximum_fusion
  9.1 0.0 all-gather.2.cloned.1.call-update
  9.1 0.0 copy-done.1
  9.1 0.1 fusion.3
  9.2 0.2 reduce_window_sum.11
  9.4 0.2 select_reduce_fusion
  9.6 0.0 copy-done.2
  9.6 0.0 copy-done
  9.6 1.6 scatter_custom_fusion
  11.2 0.2 all_to_all.15
  11.5 22.9 %all_to_all.23 = bf16[16,10,2048]{2,1,0:T(8,128)(2,1)S(1)} all-to-all(bf16[16,10,2048]{2,1,0:T(8,128)(2,1)S(1)} %all_to_all.15), channel_id=1, replica_groups=mesh['dp'=32,'expert'=16] {'expert'}, dimensions={0} | all-to-all | bytes 1310720 | tf_op jit(solution)/shard_map/all_to_all | solution.py:75
  34.4 1.1 all_to_all.17.rows_ref
  35.5 211.8 %all-gather.2.cloned.1.call-done = bf16[1,10240,2048]{2,1,0:T(8,128)(2,1)} async-done(((bf16[1,320,2048]{2,1,0:T(8,128)(2,1)}), bf16[1,10240,2048]{2,1,0:T(8,128)(2,1)}) %all-gather.2.cloned.1.call-update) | async-done | bytes 41943056 | tf_op jit(solution)/shard_map/all_gather | solution.py:81
  247.3 18.9 %shard_map.64 = bf16[160,2048]{1,0:T(8,128)(2,1)} custom-call(bf16[160,2048]{1,0:T(8,128)(2,1)} %all_to_all.17.rows_ref, bf16[160,5120]{1,0:T(8,128)(2,1)} %bitcast.11, bf16[32,2,160,2048]{3,2,1,0:T(8,128)(2,1)} %bitcast.10), custom_call_target="tpu_custom_call" | custom-call | flops 6710886400 | bytes 44892160 | tf_op jit(solution)/shard_map/pallas_call | solution.py:42
  266.2 2.2 all_to_all.18
  268.3 7.3 %all-to-all-start.1 = ((bf16[16,10,2048]{2,1,0:T(8,128)(2,1)}), bf16[16,10,2048]{2,1,0:T(8,128)(2,1)S(1)}, u32[]{:S(2)}, u32[]{:S(2)}) async-start(bf16[16,10,2048]{2,1,0:T(8,128)(2,1)} %all_to_all.18), calls=%async_computation.1 | async-start | bytes 2097152 | tf_op jit(solution)/shard_map/all_to_all | solution.py:83
  275.6 16.8 %all-to-all-done.1 = bf16[16,10,2048]{2,1,0:T(8,128)(2,1)S(1)} async-done(((bf16[16,10,2048]{2,1,0:T(8,128)(2,1)}), bf16[16,10,2048]{2,1,0:T(8,128)(2,1)S(1)}, u32[]{:S(2)}, u32[]{:S(2)}) %all-to-all-start.1) | async-done | bytes 655392 | tf_op jit(solution)/shard_map/all_to_all | solution.py:83
  292.5 0.2 all_to_all.20
  292.7 1.7 gather_fusion
  (2 shorter events, 0.0 us)
Async XLA Ops:
  6.5 2.6 copy-start.1
  6.5 3.1 %copy-start.2 = (f32[128,1]{0,1:T(1,128)S(1)}, f32[128,1]{0,1:T(1,128)}, u32[]{:S(2)}) copy-start(f32[128,1]{0,1:T(1,128)} %param.7) | copy-start | bytes 1540
  6.5 3.1 %copy-start = (bf16[128,2048]{1,0:T(8,128)(2,1)S(1)}, bf16[128,2048]{1,0:T(8,128)(2,1)}, u32[]{:S(2)}) copy-start(bf16[128,2048]{1,0:T(8,128)(2,1)} %param.6) | copy-start | bytes 1572868
  6.5 240.7 %all-gather.2.cloned.1.call-start = ((), (), s32[]{:S(2)}) async-start(), calls=%async_computation.2 | async-start | bytes 43253760 | tf_op jit(solution)/shard_map/all_gather | solution.py:81
  268.3 24.1 %all-to-all-start.1 = ((bf16[16,10,2048]{2,1,0:T(8,128)(2,1)}), bf16[16,10,2048]{2,1,0:T(8,128)(2,1)S(1)}, u32[]{:S(2)}, u32[]{:S(2)}) async-start(bf16[16,10,2048]{2,1,0:T(8,128)(2,1)} %all_to_all.18), calls=%async_computation.1 | async-start | bytes 2097152 | tf_op jit(solution)/shard_map/all_to_all | solution.py:83
Sparse Core Ops, SparseCore 0:
  9.5 237.7 all-gather.1

commit v5 on v3

--- a/solution.py
+++ b/solution.py
@@ -32,10 +32,12 @@
 
     @pl.when(step == pl.num_programs(0) - 1)
     def _():
-        out_ref[...] = acc_ref[...].astype(out_ref.dtype)
+        groups, capacity, _ = out_ref.shape
+        for j in range(groups):
+            out_ref[j] = acc_ref[j * capacity : (j + 1) * capacity, :].astype(out_ref.dtype)
 
 
-def expert_pass(rows_in, stashed, gathered, group=8):
+def expert_pass(rows_in, stashed, gathered, groups, group=8):
     shards, _, rows, width = gathered.shape
     slots = rows_in.shape[0]
     steps = shards // group
@@ -47,8 +49,8 @@
             pl.BlockSpec((slots, group * rows), lambda g: (0, g)),
             pl.BlockSpec((group, 2, rows, width), lambda g: (g, 0, 0, 0)),
         ],
-        out_specs=pl.BlockSpec((slots, width), lambda g: (0, 0)),
-        out_shape=jax.ShapeDtypeStruct((slots, width), jnp.bfloat16),
+        out_specs=pl.BlockSpec((groups, slots // groups, width), lambda g: (0, 0, 0)),
+        out_shape=jax.ShapeDtypeStruct((groups, slots // groups, width), jnp.bfloat16),
         scratch_shapes=[pltpu.VMEM((slots, width), jnp.float32)],
         compiler_params=pltpu.CompilerParams(
             dimension_semantics=("arbitrary",), vmem_limit_bytes=48 * 1024 * 1024
@@ -79,9 +81,9 @@
     rows = w_out.shape[1]
     both = jnp.concatenate([w_out, w_in], axis=1)
     gathered = lax.all_gather(both, "dp", axis=1, tiled=True).reshape(shards, 2, rows, width)
-    slot_grad = expert_pass(rows_in, stashed, gathered)
+    slot_grad = expert_pass(rows_in, stashed, gathered, groups)
     returned = lax.all_to_all(slot_grad, "expert", split_axis=0, concat_axis=0, tiled=True)
-    return returned[target]
+    return returned.reshape(slots, width)[target]
 
 
 def solution(mesh):

time: 299 us -> 299 us (level)
  no operation moved by 1% of the time
where the time goes in v5:
time: 299 us
  waiting for transfers between devices  228 us (76%)
  blocking collectives  23.2 us (8%)
  Pallas kernels  18.6 us (6%)
  between operations  13.5 us (5%)
  starting transfers between devices  7.26 us (2%)
  other arithmetic  4.6 us (2%)
  local copies, waits for them, and re-layouts  3.59 us (1%)
    all_gather x1, waiting for transfers between devices, body(): lax.all_gather(both, 'dp', axis=1, tiled=True)  211 us
    all_to_all x1, blocking collectives, body(): lax.all_to_all(outgoing, 'expert', split_axis=0, concat_axis=0, tiled=True)  23.2 us
    pallas_call x1, Pallas kernels, expert_pass(): pl.pallas_call(expert_kernel, grid=(steps,), in_specs=[pl.BlockSpec((slot...  18.6 us
    all_to_all x1, waiting for transfers between devices, body(): lax.all_to_all(slot_grad, 'expert', split_axis=0, concat_axis=0, tiled=True)  16.8 us
    all_to_all x1, starting transfers between devices, body(): lax.all_to_all(slot_grad, 'expert', split_axis=0, concat_axis=0, tiled=True)  7.26 us
  transfers between devices with their start and end apart: 2, of which 2 were waited for; matrix products, arithmetic and copies ran while one was open for 1% of the time, Pallas kernels for 0%

profile of v5, /device:TPU:8, one launch (start us, length us, event | category | flops | bytes accessed | tf_op | source)
XLA Modules:
  0.0 298.8 jit_solution(13816660420102217373)
XLA Ops:
  6.5 0.0 copy-start.2
  6.5 0.0 copy-start.3
  6.5 0.0 copy-start.1
  6.5 0.0 all-gather.2.cloned.1.call-start
  6.5 2.5 pad_maximum_fusion
  9.1 0.0 all-gather.2.cloned.1.call-update
  9.1 0.0 copy-done.2
  9.1 0.1 fusion.3
  9.2 0.2 reduce_window_sum.11
  9.4 0.2 select_reduce_fusion
  9.6 0.0 copy-done.3
  9.6 0.0 copy-done.1
  9.6 1.6 scatter_custom_fusion
  11.2 0.2 all_to_all.10
  11.4 0.0 copy-start
  11.4 23.2 %all_to_all.16 = bf16[16,10,2048]{2,1,0:T(8,128)(2,1)} all-to-all(bf16[16,10,2048]{2,1,0:T(8,128)(2,1)S(1)} %all_to_all.10), channel_id=1, replica_groups=mesh['dp'=32,'expert'=16] {'expert'}, dimensions={0} | all-to-all | bytes 1310720 | tf_op jit(solution)/shard_map/all_to_all | solution.py:77
  34.6 1.4 all_to_all.12.rows_ref
  36.0 211.2 %all-gather.2.cloned.1.call-done = bf16[1,10240,2048]{2,1,0:T(8,128)(2,1)} async-done(((bf16[1,320,2048]{2,1,0:T(8,128)(2,1)}), bf16[1,10240,2048]{2,1,0:T(8,128)(2,1)}) %all-gather.2.cloned.1.call-update) | async-done | bytes 41943056 | tf_op jit(solution)/shard_map/all_gather | solution.py:83
  247.3 0.0 copy-done
  247.3 18.6 %shard_map.64 = bf16[16,10,2048]{2,1,0:T(8,128)(2,1)} custom-call(bf16[160,2048]{1,0:T(8,128)(2,1)S(1)} %all_to_all.12.rows_ref, bf16[160,5120]{1,0:T(8,128)(2,1)S(1)} %bitcast.10, bf16[32,2,160,2048]{3,2,1,0:T(8,128)(2,1)} %bitcast.11), custom_call_target="tpu_custom_call" | custom-call | flops 6710886400 | bytes 44892160 | tf_op jit(solution)/shard_map/pallas_call | solution.py:44
  265.9 7.3 %all-to-all-start.1 = ((bf16[16,10,2048]{2,1,0:T(8,128)(2,1)}), bf16[16,10,2048]{2,1,0:T(8,128)(2,1)S(1)}, u32[]{:S(2)}, u32[]{:S(2)}) async-start(bf16[16,10,2048]{2,1,0:T(8,128)(2,1)} %shard_map.64), calls=%async_computation.1 | async-start | bytes 2097152 | tf_op jit(solution)/shard_map/all_to_all | solution.py:85
  273.2 16.8 %all-to-all-done.1 = bf16[16,10,2048]{2,1,0:T(8,128)(2,1)S(1)} async-done(((bf16[16,10,2048]{2,1,0:T(8,128)(2,1)}), bf16[16,10,2048]{2,1,0:T(8,128)(2,1)S(1)}, u32[]{:S(2)}, u32[]{:S(2)}) %all-to-all-start.1) | async-done | bytes 655392 | tf_op jit(solution)/shard_map/all_to_all | solution.py:85
  290.0 0.2 reshape.18
  290.2 1.7 gather_fusion
  (2 shorter events, 0.0 us)
Async XLA Ops:
  6.5 2.6 copy-start.2
  6.5 3.0 %copy-start.3 = (f32[128,1]{0,1:T(1,128)S(1)}, f32[128,1]{0,1:T(1,128)}, u32[]{:S(2)}) copy-start(f32[128,1]{0,1:T(1,128)} %param.7) | copy-start | bytes 1540
  6.5 3.1 %copy-start.1 = (bf16[128,2048]{1,0:T(8,128)(2,1)S(1)}, bf16[128,2048]{1,0:T(8,128)(2,1)}, u32[]{:S(2)}) copy-start(bf16[128,2048]{1,0:T(8,128)(2,1)} %param.6) | copy-start | bytes 1572868
  6.5 240.7 %all-gather.2.cloned.1.call-start = ((), (), s32[]{:S(2)}) async-start(), calls=%async_computation.2 | async-start | bytes 43253760 | tf_op jit(solution)/shard_map/all_gather | solution.py:83
  11.4 235.8 %copy-start = (bf16[1,1,160,5120]{3,2,1,0:T(8,128)(2,1)S(1)}, bf16[1,1,160,5120]{3,2,1,0:T(8,128)(2,1)}, u32[]{:S(2)}) copy-start(bf16[1,1,160,5120]{3,2,1,0:T(8,128)(2,1)} %param.11) | copy-start | bytes 4915204
  265.9 24.1 %all-to-all-start.1 = ((bf16[16,10,2048]{2,1,0:T(8,128)(2,1)}), bf16[16,10,2048]{2,1,0:T(8,128)(2,1)S(1)}, u32[]{:S(2)}, u32[]{:S(2)}) async-start(bf16[16,10,2048]{2,1,0:T(8,128)(2,1)} %shard_map.64), calls=%async_computation.1 | async-start | bytes 2097152 | tf_op jit(solution)/shard_map/all_to_all | solution.py:85
Sparse Core Ops, SparseCore 0:
  9.5 237.7 all-gather.1

commit v6 on v5

--- a/solution.py
+++ b/solution.py
@@ -14,23 +14,27 @@
     )
 
 
-def expert_kernel(rows_ref, pre_ref, w_ref, out_ref, acc_ref):
-    step = pl.program_id(0)
+def expert_kernel(rows_ref, pre_ref, w_ref, out_ref, acc_ref, act_ref):
+    block, half = pl.program_id(0), pl.program_id(1)
     group, _, rows, width = w_ref.shape
+    weights = w_ref[:, 0].reshape(group * rows, width)
 
-    @pl.when(step == 0)
+    @pl.when((block == 0) & (half == 0))
     def _():
         acc_ref[...] = jnp.zeros_like(acc_ref)
 
-    w_out = w_ref[:, 0].reshape(group * rows, width)
-    w_in = w_ref[:, 1].reshape(group * rows, width)
-    hidden = lax.dot_general(
-        rows_ref[...], w_out, (((1,), (1,)), ((), ())), preferred_element_type=jnp.float32
-    )
-    act = (hidden * gelu_slope(pre_ref[...].astype(jnp.float32))).astype(jnp.bfloat16)
-    acc_ref[...] += jnp.dot(act, w_in, preferred_element_type=jnp.float32)
+    @pl.when(half == 0)
+    def _():
+        hidden = lax.dot_general(
+            rows_ref[...], weights, (((1,), (1,)), ((), ())), preferred_element_type=jnp.float32
+        )
+        act_ref[...] = (hidden * gelu_slope(pre_ref[...].astype(jnp.float32))).astype(act_ref.dtype)
 
-    @pl.when(step == pl.num_programs(0) - 1)
+    @pl.when(half == 1)
+    def _():
+        acc_ref[...] += jnp.dot(act_ref[...], weights, preferred_element_type=jnp.float32)
+
+    @pl.when((block == pl.num_programs(0) - 1) & (half == 1))
     def _():
         groups, capacity, _ = out_ref.shape
         for j in range(groups):
@@ -43,17 +47,20 @@
     steps = shards // group
     return pl.pallas_call(
         expert_kernel,
-        grid=(steps,),
+        grid=(steps, 2),
         in_specs=[
-            pl.BlockSpec((slots, width), lambda g: (0, 0)),
-            pl.BlockSpec((slots, group * rows), lambda g: (0, g)),
-            pl.BlockSpec((group, 2, rows, width), lambda g: (g, 0, 0, 0)),
+            pl.BlockSpec((slots, width), lambda g, h: (0, 0)),
+            pl.BlockSpec((slots, group * rows), lambda g, h: (0, g)),
+            pl.BlockSpec((group, 1, rows, width), lambda g, h: (g, h, 0, 0)),
         ],
-        out_specs=pl.BlockSpec((groups, slots // groups, width), lambda g: (0, 0, 0)),
+        out_specs=pl.BlockSpec((groups, slots // groups, width), lambda g, h: (0, 0, 0)),
         out_shape=jax.ShapeDtypeStruct((groups, slots // groups, width), jnp.bfloat16),
-        scratch_shapes=[pltpu.VMEM((slots, width), jnp.float32)],
+        scratch_shapes=[
+            pltpu.VMEM((slots, width), jnp.float32),
+            pltpu.VMEM((slots, group * rows), jnp.bfloat16),
+        ],
         compiler_params=pltpu.CompilerParams(
-            dimension_semantics=("arbitrary",), vmem_limit_bytes=48 * 1024 * 1024
+            dimension_semantics=("arbitrary", "arbitrary"), vmem_limit_bytes=48 * 1024 * 1024
         ),
         cost_estimate=pl.CostEstimate(
             flops=4 * slots * shards * rows * width,

time: 299 us -> 303 us (1.013)
  Pallas kernels: 18.6 us -> 22.4 us
    pallas_call x1, Pallas kernels: 18.6 us -> 22.4 us  [expert_pass(): pl.pallas_call(expert_kernel, grid=(steps, 2), in_specs=[pl.BlockSpec((sl...]
where the time goes in v6:
time: 303 us
  waiting for transfers between devices  228 us (75%)
  blocking collectives  23.2 us (8%)
  Pallas kernels  22.4 us (7%)
  between operations  13.5 us (4%)
  starting transfers between devices  7.26 us (2%)
  other arithmetic  4.6 us (2%)
  local copies, waits for them, and re-layouts  3.59 us (1%)
    all_gather x1, waiting for transfers between devices, body(): lax.all_gather(both, 'dp', axis=1, tiled=True)  211 us
    all_to_all x1, blocking collectives, body(): lax.all_to_all(outgoing, 'expert', split_axis=0, concat_axis=0, tiled=True)  23.2 us
    pallas_call x1, Pallas kernels, expert_pass(): pl.pallas_call(expert_kernel, grid=(steps, 2), in_specs=[pl.BlockSpec((sl...  22.4 us
    all_to_all x1, waiting for transfers between devices, body(): lax.all_to_all(slot_grad, 'expert', split_axis=0, concat_axis=0, tiled=True)  16.8 us
    all_to_all x1, starting transfers between devices, body(): lax.all_to_all(slot_grad, 'expert', split_axis=0, concat_axis=0, tiled=True)  7.26 us
  transfers between devices with their start and end apart: 2, of which 2 were waited for; matrix products, arithmetic and copies ran while one was open for 1% of the time, Pallas kernels for 0%

profile of v6, /device:TPU:8, one launch (start us, length us, event | category | flops | bytes accessed | tf_op | source)
XLA Modules:
  0.0 302.6 jit_solution(1946234810437219164)
XLA Ops:
  6.5 0.0 copy-start.2
  6.5 0.0 copy-start.3
  6.5 0.0 copy-start.1
  6.5 0.0 all-gather.2.cloned.1.call-start
  6.5 2.5 pad_maximum_fusion
  9.1 0.0 all-gather.2.cloned.1.call-update
  9.1 0.0 copy-done.2
  9.1 0.1 fusion.3
  9.2 0.2 reduce_window_sum.11
  9.4 0.2 select_reduce_fusion
  9.6 0.0 copy-done.3
  9.6 0.0 copy-done.1
  9.6 1.6 scatter_custom_fusion
  11.2 0.2 all_to_all.10
  11.4 0.0 copy-start
  11.4 23.2 %all_to_all.16 = bf16[16,10,2048]{2,1,0:T(8,128)(2,1)} all-to-all(bf16[16,10,2048]{2,1,0:T(8,128)(2,1)S(1)} %all_to_all.10), channel_id=1, replica_groups=mesh['dp'=32,'expert'=16] {'expert'}, dimensions={0} | all-to-all | bytes 1310720 | tf_op jit(solution)/shard_map/all_to_all | solution.py:84
  34.6 1.4 all_to_all.12.rows_ref
  36.0 211.2 %all-gather.2.cloned.1.call-done = bf16[1,10240,2048]{2,1,0:T(8,128)(2,1)} async-done(((bf16[1,320,2048]{2,1,0:T(8,128)(2,1)}), bf16[1,10240,2048]{2,1,0:T(8,128)(2,1)}) %all-gather.2.cloned.1.call-update) | async-done | bytes 41943056 | tf_op jit(solution)/shard_map/all_gather | solution.py:90
  247.3 0.0 copy-done
  247.3 22.4 %shard_map.64 = bf16[16,10,2048]{2,1,0:T(8,128)(2,1)} custom-call(bf16[160,2048]{1,0:T(8,128)(2,1)S(1)} %all_to_all.12.rows_ref, bf16[160,5120]{1,0:T(8,128)(2,1)S(1)} %bitcast.10, bf16[32,2,160,2048]{3,2,1,0:T(8,128)(2,1)} %bitcast.11), custom_call_target="tpu_custom_call" | custom-call | flops 6710886400 | bytes 44892160 | tf_op jit(solution)/shard_map/pallas_call | solution.py:48
  269.7 7.3 %all-to-all-start.1 = ((bf16[16,10,2048]{2,1,0:T(8,128)(2,1)}), bf16[16,10,2048]{2,1,0:T(8,128)(2,1)S(1)}, u32[]{:S(2)}, u32[]{:S(2)}) async-start(bf16[16,10,2048]{2,1,0:T(8,128)(2,1)} %shard_map.64), calls=%async_computation.1 | async-start | bytes 2097152 | tf_op jit(solution)/shard_map/all_to_all | solution.py:92
  277.0 16.8 %all-to-all-done.1 = bf16[16,10,2048]{2,1,0:T(8,128)(2,1)S(1)} async-done(((bf16[16,10,2048]{2,1,0:T(8,128)(2,1)}), bf16[16,10,2048]{2,1,0:T(8,128)(2,1)S(1)}, u32[]{:S(2)}, u32[]{:S(2)}) %all-to-all-start.1) | async-done | bytes 655392 | tf_op jit(solution)/shard_map/all_to_all | solution.py:92
  293.8 0.2 reshape.18
  294.1 1.7 gather_fusion
  (2 shorter events, 0.0 us)
Async XLA Ops:
  6.5 2.6 copy-start.2
  6.5 3.0 %copy-start.3 = (f32[128,1]{0,1:T(1,128)S(1)}, f32[128,1]{0,1:T(1,128)}, u32[]{:S(2)}) copy-start(f32[128,1]{0,1:T(1,128)} %param.7) | copy-start | bytes 1540
  6.5 3.1 %copy-start.1 = (bf16[128,2048]{1,0:T(8,128)(2,1)S(1)}, bf16[128,2048]{1,0:T(8,128)(2,1)}, u32[]{:S(2)}) copy-start(bf16[128,2048]{1,0:T(8,128)(2,1)} %param.6) | copy-start | bytes 1572868
  6.5 240.7 %all-gather.2.cloned.1.call-start = ((), (), s32[]{:S(2)}) async-start(), calls=%async_computation.2 | async-start | bytes 43253760 | tf_op jit(solution)/shard_map/all_gather | solution.py:90
  11.4 235.8 %copy-start = (bf16[1,1,160,5120]{3,2,1,0:T(8,128)(2,1)S(1)}, bf16[1,1,160,5120]{3,2,1,0:T(8,128)(2,1)}, u32[]{:S(2)}) copy-start(bf16[1,1,160,5120]{3,2,1,0:T(8,128)(2,1)} %param.11) | copy-start | bytes 4915204
  269.7 24.1 %all-to-all-start.1 = ((bf16[16,10,2048]{2,1,0:T(8,128)(2,1)}), bf16[16,10,2048]{2,1,0:T(8,128)(2,1)S(1)}, u32[]{:S(2)}, u32[]{:S(2)}) async-start(bf16[16,10,2048]{2,1,0:T(8,128)(2,1)} %shard_map.64), calls=%async_computation.1 | async-start | bytes 2097152 | tf_op jit(solution)/shard_map/all_to_all | solution.py:92
Sparse Core Ops, SparseCore 0:
  9.5 237.7 all-gather.1

commit v7 on v5

--- a/solution.py
+++ b/solution.py
@@ -14,16 +14,15 @@
     )
 
 
-def expert_kernel(rows_ref, pre_ref, w_ref, out_ref, acc_ref):
+def expert_kernel(rows_ref, pre_ref, wo_ref, wi_ref, out_ref, acc_ref):
     step = pl.program_id(0)
-    group, _, rows, width = w_ref.shape
 
     @pl.when(step == 0)
     def _():
         acc_ref[...] = jnp.zeros_like(acc_ref)
 
-    w_out = w_ref[:, 0].reshape(group * rows, width)
-    w_in = w_ref[:, 1].reshape(group * rows, width)
+    w_out = wo_ref[0]
+    w_in = wi_ref[0]
     hidden = lax.dot_general(
         rows_ref[...], w_out, (((1,), (1,)), ((), ())), preferred_element_type=jnp.float32
     )
@@ -37,17 +36,18 @@
             out_ref[j] = acc_ref[j * capacity : (j + 1) * capacity, :].astype(out_ref.dtype)
 
 
-def expert_pass(rows_in, stashed, gathered, groups, group=8):
-    shards, _, rows, width = gathered.shape
+def expert_pass(rows_in, stashed, gathered, groups, rows, group=8):
+    _, hidden_units, width = gathered.shape
     slots = rows_in.shape[0]
-    steps = shards // group
+    steps = hidden_units // (group * rows)
     return pl.pallas_call(
         expert_kernel,
         grid=(steps,),
         in_specs=[
             pl.BlockSpec((slots, width), lambda g: (0, 0)),
             pl.BlockSpec((slots, group * rows), lambda g: (0, g)),
-            pl.BlockSpec((group, 2, rows, width), lambda g: (g, 0, 0, 0)),
+            pl.BlockSpec((1, group * rows, width), lambda g: (0, g, 0)),
+            pl.BlockSpec((1, group * rows, width), lambda g: (1, g, 0)),
         ],
         out_specs=pl.BlockSpec((groups, slots // groups, width), lambda g: (0, 0, 0)),
         out_shape=jax.ShapeDtypeStruct((groups, slots // groups, width), jnp.bfloat16),
@@ -56,11 +56,11 @@
             dimension_semantics=("arbitrary",), vmem_limit_bytes=48 * 1024 * 1024
         ),
         cost_estimate=pl.CostEstimate(
-            flops=4 * slots * shards * rows * width,
-            transcendentals=slots * shards * rows,
+            flops=4 * slots * hidden_units * width,
+            transcendentals=slots * hidden_units,
             bytes_accessed=2 * (gathered.size + stashed.size + 2 * rows_in.size),
         ),
-    )(rows_in, stashed, gathered)
+    )(rows_in, stashed, gathered, gathered)
 
 
 def body(grad_out, gate, expert_ids, w_in, w_out, pre_act):
@@ -79,9 +79,9 @@
     stashed = pre_act[0, 0]
     shards = lax.axis_size("dp")
     rows = w_out.shape[1]
-    both = jnp.concatenate([w_out, w_in], axis=1)
-    gathered = lax.all_gather(both, "dp", axis=1, tiled=True).reshape(shards, 2, rows, width)
-    slot_grad = expert_pass(rows_in, stashed, gathered, groups)
+    both = jnp.concatenate([w_out, w_in], axis=0)
+    gathered = lax.all_gather(both, "dp", axis=1, tiled=True)
+    slot_grad = expert_pass(rows_in, stashed, gathered, groups, rows)
     returned = lax.all_to_all(slot_grad, "expert", split_axis=0, concat_axis=0, tiled=True)
     return returned.reshape(slots, width)[target]
 

time: 299 us -> 299 us (level)
  no operation moved by 1% of the time
where the time goes in v7:
time: 299 us
  waiting for transfers between devices  229 us (77%)
  blocking collectives  22.9 us (8%)
  Pallas kernels  18.7 us (6%)
  between operations  13.5 us (5%)
  starting transfers between devices  7.27 us (2%)
  other arithmetic  4.51 us (2%)
  local copies, waits for them, and re-layouts  3.03 us (1%)
    all_gather x1, waiting for transfers between devices, body(): gathered = lax.all_gather(both, 'dp', axis=1, tiled=True)  212 us
    all_to_all x1, blocking collectives, body(): lax.all_to_all(outgoing, 'expert', split_axis=0, concat_axis=0, tiled=True)  22.9 us
    pallas_call x1, Pallas kernels, expert_pass(): pl.pallas_call(expert_kernel, grid=(steps,), in_specs=[pl.BlockSpec((slot...  18.7 us
    all_to_all x1, waiting for transfers between devices, body(): lax.all_to_all(slot_grad, 'expert', split_axis=0, concat_axis=0, tiled=True)  16.8 us
    all_to_all x1, starting transfers between devices, body(): lax.all_to_all(slot_grad, 'expert', split_axis=0, concat_axis=0, tiled=True)  7.27 us
  transfers between devices with their start and end apart: 2, of which 2 were waited for; matrix products, arithmetic and copies ran while one was open for 1% of the time, Pallas kernels for 0%

profile of v7, /device:TPU:8, one launch (start us, length us, event | category | flops | bytes accessed | tf_op | source)
XLA Modules:
  0.0 298.9 jit_solution(7600747227789030871)
XLA Ops:
  6.5 0.0 all-gather.2.cloned.1.call-start
  6.5 2.5 pad_maximum_fusion
  9.0 0.0 copy-start.2
  9.0 0.0 copy-start.1
  9.0 0.0 copy-start.3
  9.0 0.0 all-gather.2.cloned.1.call-update
  9.0 0.6 copy-done.2
  9.7 0.1 fusion.3
  9.7 0.2 reduce_window_sum.11
  9.9 0.2 select_reduce_fusion
  10.1 0.0 copy-done.1
  10.1 0.0 copy-done.3
  10.1 1.6 scatter_custom_fusion
  11.7 0.2 all_to_all.10
  12.0 22.9 %all_to_all.16 = bf16[16,10,2048]{2,1,0:T(8,128)(2,1)S(1)} all-to-all(bf16[16,10,2048]{2,1,0:T(8,128)(2,1)S(1)} %all_to_all.10), channel_id=1, replica_groups=mesh['dp'=32,'expert'=16] {'expert'}, dimensions={0} | all-to-all | bytes 1310720 | tf_op jit(solution)/shard_map/all_to_all | solution.py:77
  34.9 0.0 copy-start
  34.9 0.2 all_to_all.12.rows_ref
  35.1 212.1 %all-gather.2.cloned.1.call-done.wo_ref.wi_ref = bf16[2,5120,2048]{2,1,0:T(8,128)(2,1)} async-done(((bf16[2,160,2048]{2,1,0:T(8,128)(2,1)}), bf16[2,5120,2048]{2,1,0:T(8,128)(2,1)}) %all-gather.2.cloned.1.call-update) | async-done | bytes 41943056 | tf_op jit(solution)/shard_map/all_gather | solution.py:83
  247.3 0.0 copy-done
  247.3 18.7 %shard_map.64 = bf16[16,10,2048]{2,1,0:T(8,128)(2,1)} custom-call(bf16[160,2048]{1,0:T(8,128)(2,1)S(1)} %all_to_all.12.rows_ref, bf16[160,5120]{1,0:T(8,128)(2,1)S(1)} %bitcast.9, bf16[2,5120,2048]{2,1,0:T(8,128)(2,1)} %all-gather.2.cloned.1.call-done.wo_ref.wi_ref, bf16[2,5120,2048]{2,1,0:T(8,128)(2,1)} %all-gather.2.cloned.1.call-done.wo_ref.wi_ref), custom_call_target="tpu_custom_call" | custom-call | flops 6710886400 | bytes 44892160 | tf_op jit(solution)/shard_map/pallas_call | solution.py:43
  266.0 7.3 %all-to-all-start.1 = ((bf16[16,10,2048]{2,1,0:T(8,128)(2,1)}), bf16[16,10,2048]{2,1,0:T(8,128)(2,1)S(1)}, u32[]{:S(2)}, u32[]{:S(2)}) async-start(bf16[16,10,2048]{2,1,0:T(8,128)(2,1)} %shard_map.64), calls=%async_computation.1 | async-start | bytes 2097152 | tf_op jit(solution)/shard_map/all_to_all | solution.py:85
  273.3 16.8 %all-to-all-done.1 = bf16[16,10,2048]{2,1,0:T(8,128)(2,1)S(1)} async-done(((bf16[16,10,2048]{2,1,0:T(8,128)(2,1)}), bf16[16,10,2048]{2,1,0:T(8,128)(2,1)S(1)}, u32[]{:S(2)}, u32[]{:S(2)}) %all-to-all-start.1) | async-done | bytes 655392 | tf_op jit(solution)/shard_map/all_to_all | solution.py:85
  290.1 0.2 reshape.14
  290.4 1.7 gather_fusion
  (2 shorter events, 0.0 us)
Async XLA Ops:
  6.5 240.7 %all-gather.2.cloned.1.call-start = ((), (), s32[]{:S(2)}) async-start(), calls=%async_computation.2 | async-start | bytes 43253760 | tf_op jit(solution)/shard_map/all_gather | solution.py:83
  9.0 0.7 copy-start.2
  9.0 1.1 copy-start.1
  9.0 1.1 copy-start.3
  34.9 212.4 %copy-start = (bf16[1,1,160,5120]{3,2,1,0:T(8,128)(2,1)S(1)}, bf16[1,1,160,5120]{3,2,1,0:T(8,128)(2,1)}, u32[]{:S(2)}) copy-start(bf16[1,1,160,5120]{3,2,1,0:T(8,128)(2,1)} %param.11) | copy-start | bytes 4915204
  266.0 24.1 %all-to-all-start.1 = ((bf16[16,10,2048]{2,1,0:T(8,128)(2,1)}), bf16[16,10,2048]{2,1,0:T(8,128)(2,1)S(1)}, u32[]{:S(2)}, u32[]{:S(2)}) async-start(bf16[16,10,2048]{2,1,0:T(8,128)(2,1)} %shard_map.64), calls=%async_computation.1 | async-start | bytes 2097152 | tf_op jit(solution)/shard_map/all_to_all | solution.py:85
Sparse Core Ops, SparseCore 0:
  9.5 237.7 all-gather.1

commit v8 on v5

--- a/solution.py
+++ b/solution.py
@@ -27,7 +27,7 @@
     hidden = lax.dot_general(
         rows_ref[...], w_out, (((1,), (1,)), ((), ())), preferred_element_type=jnp.float32
     )
-    act = (hidden * gelu_slope(pre_ref[...].astype(jnp.float32))).astype(jnp.bfloat16)
+    act = (hidden * pre_ref[...]).astype(jnp.bfloat16)
     acc_ref[...] += jnp.dot(act, w_in, preferred_element_type=jnp.float32)
 
     @pl.when(step == pl.num_programs(0) - 1)
@@ -81,7 +81,8 @@
     rows = w_out.shape[1]
     both = jnp.concatenate([w_out, w_in], axis=1)
     gathered = lax.all_gather(both, "dp", axis=1, tiled=True).reshape(shards, 2, rows, width)
-    slot_grad = expert_pass(rows_in, stashed, gathered, groups)
+    slopes = gelu_slope(stashed.astype(jnp.float32))
+    slot_grad = expert_pass(rows_in, slopes, gathered, groups)
     returned = lax.all_to_all(slot_grad, "expert", split_axis=0, concat_axis=0, tiled=True)
     return returned.reshape(slots, width)[target]
 

time: 299 us -> 300 us (level)
  blocking collectives: 23.2 us -> 0 us
  starting transfers between devices: 7.26 us -> 17.1 us
  waiting for transfers between devices: 228 us -> 236 us
  local copies, waits for them, and re-layouts: 3.59 us -> 7.31 us
  other arithmetic: 4.6 us -> 8.04 us
    all_to_all x1 -> x0, blocking collectives: 23.2 us -> none  [body(): lax.all_to_all(outgoing, 'expert', split_axis=0, concat_axis=0, tiled=True)]
    all_to_all x0 -> x1, waiting for transfers between devices: none -> 10 us  [body(): lax.all_to_all(outgoing, 'expert', split_axis=0, concat_axis=0, tiled=True)]
    all_to_all x0 -> x1, starting transfers between devices: none -> 9.86 us  [body(): lax.all_to_all(outgoing, 'expert', split_axis=0, concat_axis=0, tiled=True)]
    add x0 -> x1, other arithmetic: none -> 3.44 us  [gelu_slope(): 0.5 * (1.0 + curved)]
  transfers between devices with their start and end apart: 2 -> 3, of which waited for: 2 -> 3; matrix products, arithmetic and copies ran while one was open for 1% -> 2% of each run, Pallas kernels for 0% -> 0%
where the time goes in v8:
time: 300 us
  waiting for transfers between devices  236 us (79%)
  Pallas kernels  17.6 us (6%)
  starting transfers between devices  17.1 us (6%)
  between operations  13.5 us (4%)
  other arithmetic  8.04 us (3%)
  local copies, waits for them, and re-layouts  7.31 us (2%)
    all_gather x1, waiting for transfers between devices, body(): lax.all_gather(both, 'dp', axis=1, tiled=True)  209 us
    pallas_call x1, Pallas kernels, expert_pass(): pl.pallas_call(expert_kernel, grid=(steps,), in_specs=[pl.BlockSpec((slot...  17.6 us
    all_to_all x1, waiting for transfers between devices, body(): lax.all_to_all(slot_grad, 'expert', split_axis=0, concat_axis=0, tiled=True)  16.8 us
    all_to_all x1, waiting for transfers between devices, body(): lax.all_to_all(outgoing, 'expert', split_axis=0, concat_axis=0, tiled=True)  10 us
    all_to_all x1, starting transfers between devices, body(): lax.all_to_all(outgoing, 'expert', split_axis=0, concat_axis=0, tiled=True)  9.86 us
    all_to_all x1, starting transfers between devices, body(): lax.all_to_all(slot_grad, 'expert', split_axis=0, concat_axis=0, tiled=True)  7.25 us
  transfers between devices with their start and end apart: 3, of which 3 were waited for; matrix products, arithmetic and copies ran while one was open for 2% of the time, Pallas kernels for 0%

profile of v8, /device:TPU:8, one launch (start us, length us, event | category | flops | bytes accessed | tf_op | source)
XLA Modules:
  0.0 299.9 jit_solution(16248425627478688540)
XLA Ops:
  6.5 0.0 copy-start.3
  6.5 0.0 copy-start.4
  6.5 0.0 copy-start.2
  6.5 0.0 all-gather.2.cloned.1.call-start
  6.5 2.6 pad_maximum_fusion
  9.1 0.0 all-gather.2.cloned.1.call-update
  9.1 0.0 copy-done.3
  9.1 0.1 fusion.10
  9.2 0.2 reduce_window_sum.11
  9.4 0.2 select_reduce_fusion
  9.6 0.0 copy-done.4
  9.6 0.0 copy-done.2
  9.6 1.6 scatter_custom_fusion
  11.2 1.2 all_to_all.10
  12.4 9.9 %all-to-all-start = ((bf16[16,10,2048]{2,1,0:T(8,128)(2,1)}), bf16[16,10,2048]{2,1,0:T(8,128)(2,1)}, u32[]{:S(2)}, u32[]{:S(2)}) async-start(bf16[16,10,2048]{2,1,0:T(8,128)(2,1)} %all_to_all.10), calls=%async_computation | async-start | bytes 2097152 | tf_op jit(solution)/shard_map/all_to_all | solution.py:77
  22.2 3.4 %fusion.5.pre_ref = f32[160,5120]{1,0:T(8,128)S(1)} fusion(bf16[1,1,160,5120]{3,2,1,0:T(8,128)(2,1)} %param.11), kind=kLoop, calls=%fused_computation.14 | loop fusion | flops 14745600 | bytes 4915200 | tf_op jit(solution)/shard_map/add | solution.py:12
  25.7 10.0 %all-to-all-done = bf16[16,10,2048]{2,1,0:T(8,128)(2,1)} async-done(((bf16[16,10,2048]{2,1,0:T(8,128)(2,1)}), bf16[16,10,2048]{2,1,0:T(8,128)(2,1)}, u32[]{:S(2)}, u32[]{:S(2)}) %all-to-all-start) | async-done | bytes 655392 | tf_op jit(solution)/shard_map/all_to_all | solution.py:77
  35.7 2.1 all_to_all.12.rows_ref
  37.8 209.4 %all-gather.2.cloned.1.call-done = bf16[1,10240,2048]{2,1,0:T(8,128)(2,1)} async-done(((bf16[1,320,2048]{2,1,0:T(8,128)(2,1)}), bf16[1,10240,2048]{2,1,0:T(8,128)(2,1)}) %all-gather.2.cloned.1.call-update) | async-done | bytes 41943056 | tf_op jit(solution)/shard_map/all_gather | solution.py:83
  247.3 0.0 copy-start.1
  247.3 1.1 copy-done.1
  248.4 17.6 %shard_map.64 = bf16[16,10,2048]{2,1,0:T(8,128)(2,1)S(1)} custom-call(bf16[160,2048]{1,0:T(8,128)(2,1)S(1)} %copy-done.1, f32[160,5120]{1,0:T(8,128)S(1)} %fusion.5.pre_ref, bf16[32,2,160,2048]{3,2,1,0:T(8,128)(2,1)} %bitcast.13), custom_call_target="tpu_custom_call" | custom-call | flops 6710886400 | bytes 44892160 | tf_op jit(solution)/shard_map/pallas_call | solution.py:44
  266.0 0.0 copy-start
  266.0 1.0 copy-done
  267.0 7.3 %all-to-all-start.1 = ((bf16[16,10,2048]{2,1,0:T(8,128)(2,1)}), bf16[16,10,2048]{2,1,0:T(8,128)(2,1)S(1)}, u32[]{:S(2)}, u32[]{:S(2)}) async-start(bf16[16,10,2048]{2,1,0:T(8,128)(2,1)} %copy-done), calls=%async_computation.1 | async-start | bytes 2097152 | tf_op jit(solution)/shard_map/all_to_all | solution.py:86
  274.2 16.8 %all-to-all-done.1 = bf16[16,10,2048]{2,1,0:T(8,128)(2,1)S(1)} async-done(((bf16[16,10,2048]{2,1,0:T(8,128)(2,1)}), bf16[16,10,2048]{2,1,0:T(8,128)(2,1)S(1)}, u32[]{:S(2)}, u32[]{:S(2)}) %all-to-all-start.1) | async-done | bytes 655392 | tf_op jit(solution)/shard_map/all_to_all | solution.py:86
  291.1 0.2 reshape.20
  291.3 1.7 gather_fusion
  (2 shorter events, 0.0 us)
Async XLA Ops:
  6.5 2.6 copy-start.3
  6.5 3.1 %copy-start.4 = (f32[128,1]{0,1:T(1,128)S(1)}, f32[128,1]{0,1:T(1,128)}, u32[]{:S(2)}) copy-start(f32[128,1]{0,1:T(1,128)} %param.7) | copy-start | bytes 1540
  6.5 3.1 %copy-start.2 = (bf16[128,2048]{1,0:T(8,128)(2,1)S(1)}, bf16[128,2048]{1,0:T(8,128)(2,1)}, u32[]{:S(2)}) copy-start(bf16[128,2048]{1,0:T(8,128)(2,1)} %param.6) | copy-start | bytes 1572868
  6.5 240.7 %all-gather.2.cloned.1.call-start = ((), (), s32[]{:S(2)}) async-start(), calls=%async_computation.2 | async-start | bytes 43253760 | tf_op jit(solution)/shard_map/all_gather | solution.py:83
  12.4 23.3 %all-to-all-start = ((bf16[16,10,2048]{2,1,0:T(8,128)(2,1)}), bf16[16,10,2048]{2,1,0:T(8,128)(2,1)}, u32[]{:S(2)}, u32[]{:S(2)}) async-start(bf16[16,10,2048]{2,1,0:T(8,128)(2,1)} %all_to_all.10), calls=%async_computation | async-start | bytes 2097152 | tf_op jit(solution)/shard_map/all_to_all | solution.py:77
  247.3 1.1 copy-start.1
  266.0 1.0 copy-start
  267.0 24.1 %all-to-all-start.1 = ((bf16[16,10,2048]{2,1,0:T(8,128)(2,1)}), bf16[16,10,2048]{2,1,0:T(8,128)(2,1)S(1)}, u32[]{:S(2)}, u32[]{:S(2)}) async-start(bf16[16,10,2048]{2,1,0:T(8,128)(2,1)} %copy-done), calls=%async_computation.1 | async-start | bytes 2097152 | tf_op jit(solution)/shard_map/all_to_all | solution.py:86
Sparse Core Ops, SparseCore 0:
  9.5 237.7 all-gather.1
